TPU v7x, 128 devices: a whole 4x4x4 slice. The times are simulated.
128 devices in a mesh: ctx: 8 (over y, core), head: 16 (over z, x).
Axes of the slice: x: 4, y: 4, z: 4, core: 2. Of those that a mesh axis runs over, the one named last changes fastest.
Arguments:
- conv_input: bfloat16 [32768, 20480], P(('ctx', 'head')), may hold values from -6 to 6
- dt_raw: bfloat16 [32768, 256], P(('ctx', 'head')), as said below
- conv_weight: bfloat16 [4, 20480], replicated, may hold values from -3 to 3
- conv_bias: float32 [20480], replicated, may hold values from -3 to 3
- a_log: float32 [256], replicated, may hold values from -0.2 to 0.2
- dt_bias: float32 [256], replicated, as said below
- d_skip: float32 [256], replicated, may hold values from 0.5 to 1.5
Outputs:
- scan_out: bfloat16 [32768, 16384], P('ctx', 'head')
Inputs may be any that keep to these rules, and one draw needn't show every extreme that they name: softplus(dt_bias[h]) lies between 0.02 / 32768 and 0.04 for every head. softplus(dt_raw[t, h] + dt_bias[h]) lies between 0.02 / 32768 and 0.5 for every token and head.
All inputs are finite; a program needn't handle non-finite values.
Results may differ from a plain program's by a relative error of at most 0.0046.
Values may be sent and summed in bfloat16 or wider, within the bound.
No kernel may reach another device: no remote copies, remote signals or barrier semaphores. Data moves between devices by JAX's collectives and lax.ppermute only.
A program may use at most 256 MiB of HBM per device.

v0:
```python
import jax
import jax.numpy as jnp
from jax import lax
from jax.sharding import PartitionSpec as P

HEADS = 256
HEADDIM = 64
STATE = 256
GROUPS = 8
CONV = 4
SPAN = 512


def shifted(value, axis, by):
    size = lax.axis_size(axis)
    pairs = [(i, i + by) for i in range(size) if 0 <= i + by < size]
    return lax.ppermute(value, axis, pairs)


def prefix(value, axis, combine, identity):
    size, position = (lax.axis_size(axis), lax.axis_index(axis))
    everything = jax.tree.map(lambda part: lax.all_gather(part, axis), value)
    start = jax.tree.map(
        lambda part, zero: jnp.broadcast_to(jnp.asarray(zero, part.dtype), part.shape),
        value,
        identity,
    )

    def turn(k, before):
        reached = k < position
        new = combine(before, jax.tree.map(lambda part: part[k], everything))
        return jax.tree.map(lambda a, b: jnp.where(reached, a, b), new, before)

    return lax.fori_loop(0, size, turn, start)


def compose(earlier, later):
    fade = jnp.exp(jnp.repeat(later[1], HEADDIM, axis=-1))
    return (earlier[0] * fade[..., None, :] + later[0], earlier[1] + later[1])


def on_device(conv_input, dt_raw, conv_weight, conv_bias, a_log, dt_bias, d_skip):
    f32 = jnp.float32
    head_count = lax.axis_size("head")
    heads_dev = HEADS // head_count
    repeat_count = head_count // GROUPS
    head_pos = lax.axis_index("head")
    group = head_pos // repeat_count
    rows = conv_input.shape[0]
    x_width = HEADS * HEADDIM
    slab = heads_dev * HEADDIM
    x_part = conv_input[:, :x_width].reshape(rows, head_count, slab)
    step_part = dt_raw.reshape(rows, head_count, heads_dev)
    arrived, steps = (
        lax.all_to_all(x_part, "head", split_axis=1, concat_axis=0, tiled=True),
        lax.all_to_all(step_part, "head", split_axis=1, concat_axis=0, tiled=True),
    )
    length = arrived.shape[0]
    shared = lax.all_gather(conv_input[:, x_width:], "head", axis=0, tiled=True)
    b_cols = lax.dynamic_slice_in_dim(shared, group * STATE, STATE, 1)
    c_cols = lax.dynamic_slice_in_dim(shared, (GROUPS + group) * STATE, STATE, 1)
    local = jnp.concatenate([arrived.reshape(length, slab), b_cols, c_cols], 1)
    steps = steps.reshape(length, heads_dev)

    def columns(table):
        last = table.ndim - 1
        return jnp.concatenate(
            [
                lax.dynamic_slice_in_dim(table, head_pos * slab, slab, last),
                lax.dynamic_slice_in_dim(table, x_width + group * STATE, STATE, last),
                lax.dynamic_slice_in_dim(table, x_width + (GROUPS + group) * STATE, STATE, last),
            ],
            last,
        )

    kernel = columns(conv_weight).astype(f32)
    offset = columns(conv_bias)
    rim = shifted(local[length - (CONV - 1) :], "ctx", 1)
    padded = jnp.concatenate([rim, local], 0)
    total = padded[0:length].astype(f32) * kernel[0]
    for k in range(1, CONV):
        total = total + padded[k : k + length].astype(f32) * kernel[k]
    act = jax.nn.silu(total + offset).astype(jnp.bfloat16)
    rate = -jnp.exp(lax.dynamic_slice_in_dim(a_log, head_pos * heads_dev, heads_dev, 0))
    bias = lax.dynamic_slice_in_dim(dt_bias, head_pos * heads_dev, heads_dev, 0)
    skip = jnp.repeat(lax.dynamic_slice_in_dim(d_skip, head_pos * heads_dev, heads_dev, 0), HEADDIM)
    step = jax.nn.softplus(steps.astype(f32) + bias)
    blocks = length // SPAN
    x_blocks = act[:, :slab].reshape(blocks, SPAN, slab)
    b_blocks = act[:, slab : slab + STATE].reshape(blocks, SPAN, STATE)
    c_blocks = act[:, slab + STATE :].reshape(blocks, SPAN, STATE)
    step_blocks = step.reshape(blocks, SPAN, heads_dev)
    cum = jnp.cumsum((rate * step).reshape(blocks, SPAN, heads_dev), axis=1)
    tri = lax.broadcasted_iota(jnp.int32, (SPAN, SPAN), 0) >= lax.broadcasted_iota(
        jnp.int32, (SPAN, SPAN), 1
    )

    def local_block(state, inputs):
        x_now, b_now, c_now, step_now, cum_now = inputs
        gram = jnp.dot(c_now, b_now.T, preferred_element_type=f32)
        cum_t = cum_now.T
        decay = jnp.exp(jnp.where(tri[None], cum_t[:, :, None] - cum_t[:, None, :], -jnp.inf))
        mix = (gram[None] * decay * step_now.T[:, None, :]).astype(jnp.bfloat16)
        x_heads = x_now.reshape(SPAN, heads_dev, HEADDIM)
        y_block = jnp.einsum("hts,shp->thp", mix, x_heads, preferred_element_type=f32).reshape(
            SPAN, slab
        )
        weight = jnp.exp(cum_now[-1][None, :] - cum_now) * step_now
        xw = (x_heads.astype(f32) * weight[:, :, None]).astype(jnp.bfloat16).reshape(SPAN, slab)
        contrib = jnp.einsum("sn,sc->nc", b_now, xw, preferred_element_type=f32)
        fade = jnp.exp(jnp.repeat(cum_now[-1], HEADDIM))
        return (state * fade[None, :] + contrib, (y_block, state))

    start_state = jnp.zeros((STATE, slab), f32)
    final, (y_blocks, entering) = lax.scan(
        local_block, start_state, (x_blocks, b_blocks, c_blocks, step_blocks, cum)
    )
    block_totals = cum[:, -1, :]
    totals = jnp.sum(block_totals, axis=0)
    incoming, passed = prefix(
        (final, totals),
        "ctx",
        compose,
        (jnp.zeros((STATE, slab), f32), jnp.zeros((heads_dev,), f32)),
    )
    before = jnp.concatenate(
        [jnp.zeros((1, heads_dev), f32), jnp.cumsum(block_totals, axis=0)[:-1]], 0
    )
    carried = jnp.exp(jnp.repeat(before, HEADDIM, axis=1))[:, None, :] * incoming[None]
    full_state = entering + carried
    grown = jnp.exp(jnp.repeat(cum, HEADDIM, axis=2))
    y_state = grown * jnp.einsum(
        "bqn,bnc->bqc", c_blocks.astype(f32), full_state, precision=lax.Precision.HIGHEST
    )
    result = y_blocks + y_state + skip * x_blocks.astype(f32)
    return result.astype(jnp.bfloat16).reshape(length, slab)


def solution(mesh):
    placed = (P(("ctx", "head"), None), P(("ctx", "head"), None), P(), P(), P(), P(), P())
    return jax.shard_map(
        on_device, mesh=mesh, in_specs=placed, out_specs=P("ctx", "head"), check_vma=False
    )
```

profile of v0, /device:TPU:1, one launch (start us, length us, event | category | flops | bytes accessed | tf_op | source)
XLA Modules:
  0.0 625.6 jit_solution(14649506826397201722)
XLA Ops:
  6.5 3.1 slice.59
  11.4 8.4 %all-to-all-start = ((bf16[256,16,16]{0,2,1:T(8,128)(2,1)}), bf16[256,16,16]{0,2,1:T(8,128)(2,1)S(1)}, u32[]{:S(2)}, u32[]{:S(2)}) async-start(bf16[256,16,16]{0,2,1:T(8,128)(2,1)} %bitcast), calls=%async_computation | async-start | bytes 262144 | tf_op jit(solution)/shard_map/all_to_all | solution.py:56
  19.8 8.5 %slice.58 = bf16[256,16384]{1,0:T(8,128)(2,1)} slice(bf16[256,20480]{1,0:T(8,128)(2,1)} %param.11), slice={[0:256], [0:16384]} | slice | bytes 16777216 | tf_op jit(solution)/shard_map/slice | solution.py:52
  28.2 12.0 %copy.62 = bf16[256,16384]{0,1:T(8,128)(2,1)} copy(bf16[256,16384]{1,0:T(8,128)(2,1)} %slice.58) | data formatting | bytes 16777216
  40.2 12.3 %copy.53 = bf16[256,16,1024]{2,0,1:T(8,128)(2,1)} copy(bf16[256,16,1024]{0,2,1:T(8,128)(2,1)} %bitcast.115) | data formatting | bytes 16777216 | tf_op jit(solution)/shard_map/reshape | solution.py:52
  52.5 6.8 %all-to-all-start.1 = ((bf16[256,16,1024]{2,0,1:T(8,128)(2,1)}), bf16[256,16,1024]{2,0,1:T(8,128)(2,1)}, u32[]{:S(2)}, u32[]{:S(2)}) async-start(bf16[256,16,1024]{2,0,1:T(8,128)(2,1)} %copy.53), calls=%async_computation.1 | async-start | bytes 16777216 | tf_op jit(solution)/shard_map/all_to_all | solution.py:55
  64.0 9.1 %reduce-window.6 = f32[8,16,4,128]{3,1,2,0:T(8,128)S(1)} reduce-window(f32[8,16,4,128]{3,1,2,0:T(8,128)S(1)} %copy.48, f32[]{:T(128)} %constant.84.clone.1), window={size=1x1x1x128 pad=0_0x0_0x0_0x127_0}, to_apply=%region_0.1 | reduce-window | flops 8323072 | bytes 524292 | tf_op jit(solution)/shard_map/reduce-window
  73.6 214.8 %all-gather.5.cloned.1.call-done = bf16[4096,4096]{1,0:T(8,128)(2,1)} async-done(((bf16[256,4096]{1,0:T(8,128)(2,1)}), bf16[4096,4096]{1,0:T(8,128)(2,1)}) %all-gather.5.cloned.1.call-update) | async-done | bytes 33554448 | tf_op jit(solution)/shard_map/all_gather | solution.py:59
  288.5 3.8 constant_dynamic-slice_fusion.6
  292.3 6.0 pad_maximum_fusion
  298.3 3.8 collective-permute-start
  302.9 7.5 %maximum_maximum_fusion = bf16[4099,1536]{1,0:T(8,128)(2,1)S(1)} fusion(bf16[4096,256]{1,0:T(8,128)(2,1)S(1)} %copy-done.2, bf16[4096,256]{1,0:T(8,128)(2,1)S(1)} %get-tuple-element.290, bf16[4096,1024]{1,0:T(8,128)(2,1)} %bitcast.10, bf16[3,1536]{1,0:T(4,128)(2,1)S(1)} %collective-permute-done), kind=kLoop, calls=%fused_computation.32 | loop fusion | flops 50368512 | bytes 25184256 | tf_op jit(solution)/shard_map/concatenate | solution.py:79
  310.4 23.0 %multiply_convert_fusion.3 = bf16[4096,1536]{1,0:T(8,128)(2,1)} fusion(bf16[4099,1536]{1,0:T(8,128)(2,1)S(1)} %maximum_maximum_fusion, f32[1536]{0:T(1024)S(1)} %pad_maximum_fusion.1, f32[1536]{0:T(1024)S(1)} %get-tuple-element.255, f32[1536]{0:T(1024)S(1)} %get-tuple-element.256, f32[1536]{0:T(1024)S(1)} %get-tuple-element.257, ...), kind=kLoop, calls=%fused_computation.30 | loop fusion | flops 138412032 | bytes 62945280 | tf_op jit(solution)/shard_map/convert_element_type | solution.py:83
  333.5 7.8 %slice.85 = bf16[4096,1024]{1,0:T(8,128)(2,1)} slice(bf16[4096,1536]{1,0:T(8,128)(2,1)} %multiply_convert_fusion.3), slice={[0:4096], [0:1024]} | slice | bytes 16777216 | tf_op jit(solution)/shard_map/slice | solution.py:89
  341.2 4.5 fusion.23
  345.7 180.6 %while.29 = (s32[]{:T(128)}, f32[256,1024]{1,0:T(8,128)S(1)}, f32[8,512,1024]{2,1,0:T(8,128)}, f32[8,256,1024]{2,1,0:T(8,128)}, f32[8,512,16]{1,2,0:T(8,128)}, /...) while((s32[]{:T(128)}, f32[256,1024]{1,0:T(8,128)S(1)}, ...), condition=%wide.region_3.4_spmd.clone, body=%wide.region_2.3_spmd.clone.sunk | while | flops 963395584 | bytes 31083584 | solution.py:115
  347.5 2.3 fusion.41
  351.7 7.1 %fusion.42 = f32[16,64,512]{2,1,0:T(8,128)} fusion(bf16[512,16,64]{0,2,1:T(8,128)(2,1)S(1)} %bitcast.110, f32[16,512]{1,0:T(8,128)S(1)} %get-tuple-element.381, f32[16,512]{1,0:T(8,128)S(1)} %get-tuple-element.382, f32[512,512]{1,0:T(8,128)} %fusion.41, pred[512,512]{1,0:T(8,128)(4,1)S(1)} %iota_compare_fusion.2), kind=kOutput, calls=%fused_computation.5.clone.1 | convolution fusion | flops 557842432 | bytes 4521984 | tf_op jit(solution)/shard_map/while/body/eval_jaxpr/hts,shp->thp/dot_general | solution.py:105
  358.8 1.9 copy.81
  370.0 2.3 fusion.41
  374.3 7.1 %fusion.42 = f32[16,64,512]{2,1,0:T(8,128)} fusion(bf16[512,16,64]{0,2,1:T(8,128)(2,1)S(1)} %bitcast.110, f32[16,512]{1,0:T(8,128)S(1)} %get-tuple-element.381, f32[16,512]{1,0:T(8,128)S(1)} %get-tuple-element.382, f32[512,512]{1,0:T(8,128)} %fusion.41, pred[512,512]{1,0:T(8,128)(4,1)S(1)} %iota_compare_fusion.2), kind=kOutput, calls=%fused_computation.5.clone.1 | convolution fusion | flops 557842432 | bytes 4521984 | tf_op jit(solution)/shard_map/while/body/eval_jaxpr/hts,shp->thp/dot_general | solution.py:105
  381.4 1.9 copy.81
  392.7 2.3 fusion.41
  396.9 7.1 %fusion.42 = f32[16,64,512]{2,1,0:T(8,128)} fusion(bf16[512,16,64]{0,2,1:T(8,128)(2,1)S(1)} %bitcast.110, f32[16,512]{1,0:T(8,128)S(1)} %get-tuple-element.381, f32[16,512]{1,0:T(8,128)S(1)} %get-tuple-element.382, f32[512,512]{1,0:T(8,128)} %fusion.41, pred[512,512]{1,0:T(8,128)(4,1)S(1)} %iota_compare_fusion.2), kind=kOutput, calls=%fused_computation.5.clone.1 | convolution fusion | flops 557842432 | bytes 4521984 | tf_op jit(solution)/shard_map/while/body/eval_jaxpr/hts,shp->thp/dot_general | solution.py:105
  415.2 2.3 fusion.41
  419.5 7.1 %fusion.42 = f32[16,64,512]{2,1,0:T(8,128)} fusion(bf16[512,16,64]{0,2,1:T(8,128)(2,1)S(1)} %bitcast.110, f32[16,512]{1,0:T(8,128)S(1)} %get-tuple-element.381, f32[16,512]{1,0:T(8,128)S(1)} %get-tuple-element.382, f32[512,512]{1,0:T(8,128)} %fusion.41, pred[512,512]{1,0:T(8,128)(4,1)S(1)} %iota_compare_fusion.2), kind=kOutput, calls=%fused_computation.5.clone.1 | convolution fusion | flops 557842432 | bytes 4521984 | tf_op jit(solution)/shard_map/while/body/eval_jaxpr/hts,shp->thp/dot_general | solution.py:105
  437.7 2.3 fusion.41
  442.0 7.1 %fusion.42 = f32[16,64,512]{2,1,0:T(8,128)} fusion(bf16[512,16,64]{0,2,1:T(8,128)(2,1)S(1)} %bitcast.110, f32[16,512]{1,0:T(8,128)S(1)} %get-tuple-element.381, f32[16,512]{1,0:T(8,128)S(1)} %get-tuple-element.382, f32[512,512]{1,0:T(8,128)} %fusion.41, pred[512,512]{1,0:T(8,128)(4,1)S(1)} %iota_compare_fusion.2), kind=kOutput, calls=%fused_computation.5.clone.1 | convolution fusion | flops 557842432 | bytes 4521984 | tf_op jit(solution)/shard_map/while/body/eval_jaxpr/hts,shp->thp/dot_general | solution.py:105
  460.3 2.3 fusion.41
  464.6 7.1 %fusion.42 = f32[16,64,512]{2,1,0:T(8,128)} fusion(bf16[512,16,64]{0,2,1:T(8,128)(2,1)S(1)} %bitcast.110, f32[16,512]{1,0:T(8,128)S(1)} %get-tuple-element.381, f32[16,512]{1,0:T(8,128)S(1)} %get-tuple-element.382, f32[512,512]{1,0:T(8,128)} %fusion.41, pred[512,512]{1,0:T(8,128)(4,1)S(1)} %iota_compare_fusion.2), kind=kOutput, calls=%fused_computation.5.clone.1 | convolution fusion | flops 557842432 | bytes 4521984 | tf_op jit(solution)/shard_map/while/body/eval_jaxpr/hts,shp->thp/dot_general | solution.py:105
  482.9 2.3 fusion.41
  487.1 7.1 %fusion.42 = f32[16,64,512]{2,1,0:T(8,128)} fusion(bf16[512,16,64]{0,2,1:T(8,128)(2,1)S(1)} %bitcast.110, f32[16,512]{1,0:T(8,128)S(1)} %get-tuple-element.381, f32[16,512]{1,0:T(8,128)S(1)} %get-tuple-element.382, f32[512,512]{1,0:T(8,128)} %fusion.41, pred[512,512]{1,0:T(8,128)(4,1)S(1)} %iota_compare_fusion.2), kind=kOutput, calls=%fused_computation.5.clone.1 | convolution fusion | flops 557842432 | bytes 4521984 | tf_op jit(solution)/shard_map/while/body/eval_jaxpr/hts,shp->thp/dot_general | solution.py:105
  505.5 2.3 fusion.41
  509.8 7.1 %fusion.42 = f32[16,64,512]{2,1,0:T(8,128)} fusion(bf16[512,16,64]{0,2,1:T(8,128)(2,1)S(1)} %bitcast.110, f32[16,512]{1,0:T(8,128)S(1)} %get-tuple-element.381, f32[16,512]{1,0:T(8,128)S(1)} %get-tuple-element.382, f32[512,512]{1,0:T(8,128)} %fusion.41, pred[512,512]{1,0:T(8,128)(4,1)S(1)} %iota_compare_fusion.2), kind=kOutput, calls=%fused_computation.5.clone.1 | convolution fusion | flops 557842432 | bytes 4521984 | tf_op jit(solution)/shard_map/while/body/eval_jaxpr/hts,shp->thp/dot_general | solution.py:105
  530.3 13.1 %all-reduce.1 = f32[128]{0:T(128)S(1)} all-reduce(f32[128]{0:T(128)S(1)} %dynamic-update-slice), channel_id=2, replica_groups=mesh['ctx'=8,'head'=16] {'ctx'}, use_global_device_ids=true, to_apply=%add.1 | all-reduce | flops 128 | bytes 1024
  543.8 8.1 %broadcast_in_dim.62 = f32[8,512,16,64]{1,3,2,0:T(8,128)} broadcast(f32[8,512,16]{1,2,0:T(8,128)S(1)} %fusion.22), dimensions={0,1,2} | broadcast | bytes 17039360 | tf_op jit(solution)/shard_map/broadcast_in_dim | solution.py:131
  551.9 16.7 %copy.56 = f32[8,512,1024]{2,1,0:T(8,128)} copy(f32[8,512,1024]{1,2,0:T(8,128)} %bitcast.112) | data formatting | bytes 33554432 | tf_op jit(solution)/shard_map/exp | solution.py:131
  568.6 9.4 %all-gather.7.cloned.1.call-done = f32[2048,1024]{1,0:T(8,128)} async-done(((f32[256,1024]{1,0:T(8,128)}), f32[2048,1024]{1,0:T(8,128)}) %all-gather.7.cloned.1.call-update) | async-done | bytes 8388624 | tf_op jit(solution)/shard_map/all_gather | solution.py:22
  578.0 18.5 %while.30 = (s32[]{:T(128)}, f32[256,1024]{1,0:T(8,128)S(1)}, s32[]{:T(128)}, f32[8,16]{1,0:T(8,128)S(1)}, f32[8,256,1024]{2,1,0:T(8,128)}, /*index=5*/s32[]{:T(128)}, s32[]{:T(128)}) while((s32[]{:T(128)}, f32[256,1024]{1,0:T(8,128)S(1)}, s32[]{:T(128)}, f32[8,16]{1,0:T(8,128)S(1)}, f32[8,256,1024]{2,1,0:T(8,128)}, ...), condition=%wide.region_7.8_spmd.clone, body=%wide.region_6.7_spmd.clone.sunk | while | flops 1048580 | bytes 3162409 | solution.py:34
  578.2 2.1 fusion.43
  580.5 2.1 fusion.43
  582.8 2.1 fusion.43
  585.1 2.1 fusion.43
  587.4 2.1 fusion.43
  589.7 2.1 fusion.43
  592.1 2.1 fusion.43
  594.4 2.1 fusion.43
  596.5 22.2 %add_convert_fusion = bf16[8,512,1024]{2,1,0:T(8,128)(2,1)} fusion(bf16[8,512,1024]{2,1,0:T(8,128)(2,1)} %get-tuple-element.449, f32[8,512,1024]{2,1,0:T(8,128)} %get-tuple-element.153, f32[8,512,1024]{2,1,0:T(8,128)} %copy.56, bf16[8,512,256]{2,1,0:T(8,128)(2,1)} %bitcast.13, f32[1024]{0:T(1024)S(1)} %mul.190, f32[8,256,1024]{2,1,0:T(8,128)} %get-tuple-element.154, ...), kind=kOutput, calls=%fused_computation.31 | convolution fusion | flops 12914262016 | bytes 61902848 | tf_op jit(solution)/shard_map/bqn,bnc->bqc/dot_general | solution.py:132
  (216 shorter events, 113.1 us)
Async XLA Ops:
  6.5 281.9 %all-gather.5.cloned.1.call-start = ((), (), s32[]{:S(2)}) async-start(), calls=%async_computation.2 | async-start | bytes 35651584 | tf_op jit(solution)/shard_map/all_gather | solution.py:59
  11.4 41.2 %all-to-all-start = ((bf16[256,16,16]{0,2,1:T(8,128)(2,1)}), bf16[256,16,16]{0,2,1:T(8,128)(2,1)S(1)}, u32[]{:S(2)}, u32[]{:S(2)}) async-start(bf16[256,16,16]{0,2,1:T(8,128)(2,1)} %bitcast), calls=%async_computation | async-start | bytes 262144 | tf_op jit(solution)/shard_map/all_to_all | solution.py:56
  52.5 7.7 %copy-start.3 = (f32[256]{0:T(256)S(1)}, f32[256]{0:T(256)}, u32[]{:S(2)}) copy-start(f32[256]{0:T(256)} %param.16) | copy-start | bytes 3076
  52.5 7.8 %copy-start.4 = (f32[256]{0:T(256)S(1)}, f32[256]{0:T(256)}, u32[]{:S(2)}) copy-start(f32[256]{0:T(256)} %param.15) | copy-start | bytes 3076
  52.5 239.8 %all-to-all-start.1 = ((bf16[256,16,1024]{2,0,1:T(8,128)(2,1)}), bf16[256,16,1024]{2,0,1:T(8,128)(2,1)}, u32[]{:S(2)}, u32[]{:S(2)}) async-start(bf16[256,16,1024]{2,0,1:T(8,128)(2,1)} %copy.53), calls=%async_computation.1 | async-start | bytes 16777216 | tf_op jit(solution)/shard_map/all_to_all | solution.py:55
  59.4 518.6 %all-gather.7.cloned.1.call-start = ((), (), s32[]{:S(2)}) async-start(), calls=%async_computation.3 | async-start | bytes 9437184 | tf_op jit(solution)/shard_map/all_gather | solution.py:22
  292.3 10.7 %copy-start.2 = (bf16[4096,256]{1,0:T(8,128)(2,1)S(1)}, bf16[4096,256]{1,0:T(8,128)(2,1)}, u32[]{:S(2)}) copy-start(bf16[4096,256]{1,0:T(8,128)(2,1)} %get-tuple-element.291) | copy-start | bytes 6291460
  298.3 4.6 collective-permute-start
  345.7 181.7 %copy-start.5 = (f32[256]{0:T(256)S(1)}, f32[256]{0:T(256)}, u32[]{:S(2)}) copy-start(f32[256]{0:T(256)} %param.17) | copy-start | bytes 3076
  345.7 181.9 %copy-start.6 = (u32[128]{0:T(128)S(1)}, u32[128]{0:T(128)}, u32[]{:S(2)}) copy-start(u32[128]{0:T(128)} %constant.103) | copy-start | bytes 1540
  351.6 7.2 %copy-start.1 = (bf16[1,512,1024]{1,2,0:T(8,128)(2,1)}, bf16[1,512,1024]{1,2,0:T(8,128)(2,1)S(1)}, u32[]{:S(2)}) copy-start(bf16[1,512,1024]{1,2,0:T(8,128)(2,1)S(1)} %copy.80) | copy-start | bytes 3145732 | tf_op jit(solution)/shard_map/while
  374.2 7.2 %copy-start.1 = (bf16[1,512,1024]{1,2,0:T(8,128)(2,1)}, bf16[1,512,1024]{1,2,0:T(8,128)(2,1)S(1)}, u32[]{:S(2)}) copy-start(bf16[1,512,1024]{1,2,0:T(8,128)(2,1)S(1)} %copy.80) | copy-start | bytes 3145732 | tf_op jit(solution)/shard_map/while
  396.8 7.2 %copy-start.1 = (bf16[1,512,1024]{1,2,0:T(8,128)(2,1)}, bf16[1,512,1024]{1,2,0:T(8,128)(2,1)S(1)}, u32[]{:S(2)}) copy-start(bf16[1,512,1024]{1,2,0:T(8,128)(2,1)S(1)} %copy.80) | copy-start | bytes 3145732 | tf_op jit(solution)/shard_map/while
  419.4 7.2 %copy-start.1 = (bf16[1,512,1024]{1,2,0:T(8,128)(2,1)}, bf16[1,512,1024]{1,2,0:T(8,128)(2,1)S(1)}, u32[]{:S(2)}) copy-start(bf16[1,512,1024]{1,2,0:T(8,128)(2,1)S(1)} %copy.80) | copy-start | bytes 3145732 | tf_op jit(solution)/shard_map/while
  441.9 7.2 %copy-start.1 = (bf16[1,512,1024]{1,2,0:T(8,128)(2,1)}, bf16[1,512,1024]{1,2,0:T(8,128)(2,1)S(1)}, u32[]{:S(2)}) copy-start(bf16[1,512,1024]{1,2,0:T(8,128)(2,1)S(1)} %copy.80) | copy-start | bytes 3145732 | tf_op jit(solution)/shard_map/while
  464.5 7.2 %copy-start.1 = (bf16[1,512,1024]{1,2,0:T(8,128)(2,1)}, bf16[1,512,1024]{1,2,0:T(8,128)(2,1)S(1)}, u32[]{:S(2)}) copy-start(bf16[1,512,1024]{1,2,0:T(8,128)(2,1)S(1)} %copy.80) | copy-start | bytes 3145732 | tf_op jit(solution)/shard_map/while
  487.1 7.2 %copy-start.1 = (bf16[1,512,1024]{1,2,0:T(8,128)(2,1)}, bf16[1,512,1024]{1,2,0:T(8,128)(2,1)S(1)}, u32[]{:S(2)}) copy-start(bf16[1,512,1024]{1,2,0:T(8,128)(2,1)S(1)} %copy.80) | copy-start | bytes 3145732 | tf_op jit(solution)/shard_map/while
  509.7 7.2 %copy-start.1 = (bf16[1,512,1024]{1,2,0:T(8,128)(2,1)}, bf16[1,512,1024]{1,2,0:T(8,128)(2,1)S(1)}, u32[]{:S(2)}) copy-start(bf16[1,512,1024]{1,2,0:T(8,128)(2,1)S(1)} %copy.80) | copy-start | bytes 3145732 | tf_op jit(solution)/shard_map/while
  526.3 1.0 copy-start
Sparse Core Ops, SparseCore 0:
  9.8 278.5 all-gather.4
  527.5 50.5 all-gather.6
where the time goes:
time: 631 us; the launch traced here: 626 us
  waiting for transfers between devices  224 us (35%)
  local copies, waits for them, and re-layouts  150 us (24%)
  matrix products  111 us (18%)
  other arithmetic  93.5 us (15%)
  starting transfers between devices  19.1 us (3%)
  between operations  14.4 us (2%)
  blocking collectives  13.1 us (2%)
    all_gather x1, waiting for transfers between devices, on_device(): shared = lax.all_gather(conv_input[:, x_width:], 'head', axis=0, tiled=True)  215 us
    dot_general x8, matrix products, local_block(): jnp.einsum('hts,shp->thp', mix, x_heads, preferred_element_type=f32)  57 us
    dynamic_update_slice x16, local copies, waits for them, and re-layouts, on_device(): lax.scan(local_block, start_state, (x_blocks, b_blocks, c_blocks, step_bl...  27.1 us
    convert_element_type x1, other arithmetic, on_device(): act = jax.nn.silu(total + offset).astype(jnp.bfloat16)  23 us
    dynamic_slice x24, local copies, waits for them, and re-layouts, on_device(): lax.scan(local_block, start_state, (x_blocks, b_blocks, c_blocks, step_bl...  22.6 us
    dot_general x1, matrix products, on_device(): jnp.einsum('bqn,bnc->bqc', c_blocks.astype(f32), full_state, precision=la...  22.2 us
    dot_general x8, matrix products, local_block(): gram = jnp.dot(c_now, b_now.T, preferred_element_type=f32)  18.5 us
    select_n x8, other arithmetic, turn(): return jax.tree.map(lambda a, b: jnp.where(reached, a, b), new, before)  17.1 us
  transfers between devices with their start and end apart: 5, of which 2 were waited for; matrix products, arithmetic and copies ran while one was open for 13% of the time, Pallas kernels for 0%

commit v1 on v0

--- a/solution.py
+++ b/solution.py
@@ -56,7 +56,11 @@
         lax.all_to_all(step_part, "head", split_axis=1, concat_axis=0, tiled=True),
     )
     length = arrived.shape[0]
-    shared = lax.all_gather(conv_input[:, x_width:], "head", axis=0, tiled=True)
+    block = conv_input[:, x_width:]
+    peers = lax.axis_size("head")
+    pieces = jnp.stack([block for _ in range(peers)])
+    pieces = lax.all_to_all(pieces, "head", split_axis=0, concat_axis=0)
+    shared = jnp.concatenate(pieces, axis=0)
     b_cols = lax.dynamic_slice_in_dim(shared, group * STATE, STATE, 1)
     c_cols = lax.dynamic_slice_in_dim(shared, (GROUPS + group) * STATE, STATE, 1)
     local = jnp.concatenate([arrived.reshape(length, slab), b_cols, c_cols], 1)

time: 631 us -> 1000 us (1.58)
  waiting for transfers between devices: 224 us -> 579 us
    all_to_all x0 -> x1, waiting for transfers between devices: none -> 463 us  [on_device(): pieces = lax.all_to_all(pieces, 'head', split_axis=0, concat_axis=0)]
    all_gather x1 -> x0, waiting for transfers between devices: 215 us -> none  [on_device(): shared = lax.all_gather(conv_input[:, x_width:], 'head', axis=0, tiled=True)]
    all_to_all x1, waiting for transfers between devices: 0.01 us -> 101 us  [on_device(): lax.all_to_all(x_part, 'head', split_axis=1, concat_axis=0, tiled=True)]
    another operation x3 -> x4, local copies, waits for them, and re-layouts: 0.17 us -> 11.1 us  [the longest x1 10.9 us: on_device(): pieces = jnp.stack([block for _ in range(peers)])]
  transfers between devices with their start and end apart: 5 -> 5, of which waited for: 2 -> 4; matrix products, arithmetic and copies ran while one was open for 13% -> 8% of each run, Pallas kernels for 0% -> 0%
where the time goes in v1:
time: 1000 us; the launch traced here: 995 us
  waiting for transfers between devices  579 us (58%)
  local copies, waits for them, and re-layouts  158 us (16%)
  matrix products  111 us (11%)
  other arithmetic  93.5 us (9%)
  starting transfers between devices  26.1 us (3%)
  between operations  14.4 us (1%)
  blocking collectives  13 us (1%)
    all_to_all x1, waiting for transfers between devices, on_device(): pieces = lax.all_to_all(pieces, 'head', split_axis=0, concat_axis=0)  463 us
    all_to_all x1, waiting for transfers between devices, on_device(): lax.all_to_all(x_part, 'head', split_axis=1, concat_axis=0, tiled=True)  101 us
    dot_general x8, matrix products, local_block(): jnp.einsum('hts,shp->thp', mix, x_heads, preferred_element_type=f32)  57 us
    dynamic_update_slice x16, local copies, waits for them, and re-layouts, on_device(): lax.scan(local_block, start_state, (x_blocks, b_blocks, c_blocks, step_bl...  27.1 us
    convert_element_type x1, other arithmetic, on_device(): act = jax.nn.silu(total + offset).astype(jnp.bfloat16)  23 us
    dynamic_slice x24, local copies, waits for them, and re-layouts, on_device(): lax.scan(local_block, start_state, (x_blocks, b_blocks, c_blocks, step_bl...  22.6 us
    dot_general x1, matrix products, on_device(): jnp.einsum('bqn,bnc->bqc', c_blocks.astype(f32), full_state, precision=la...  22.2 us
  transfers between devices with their start and end apart: 5, of which 4 were waited for; matrix products, arithmetic and copies ran while one was open for 8% of the time, Pallas kernels for 0%

profile of v1, /device:TPU:1, one launch (start us, length us, event | category | flops | bytes accessed | tf_op | source)
XLA Modules:
  0.0 995.4 jit_solution(10374806808446951511)
XLA Ops:
  8.2 8.4 all-to-all-start
  18.4 5.1 all-to-all-done
  23.5 10.9 %stack.2 = bf16[16,256,4096]{2,1,0:T(8,128)(2,1)} broadcast(bf16[256,4096]{1,0:T(8,128)(2,1)S(1)} %slice.59), dimensions={1,2} | broadcast | bytes 35651584 | tf_op jit(solution)/shard_map/stack | solution.py:61
  34.4 6.0 all-to-all-start.2
  40.4 7.7 slice.58
  48.0 11.9 %copy.62 = bf16[256,16384]{0,1:T(8,128)(2,1)} copy(bf16[256,16384]{1,0:T(8,128)(2,1)} %slice.58) | data formatting | bytes 16777216
  59.9 12.2 %copy.53 = bf16[256,16,1024]{2,0,1:T(8,128)(2,1)} copy(bf16[256,16,1024]{0,2,1:T(8,128)(2,1)} %bitcast.116) | data formatting | bytes 16777216 | tf_op jit(solution)/shard_map/reshape | solution.py:52
  72.2 463.3 %all-to-all-done.2 = bf16[16,256,4096]{2,1,0:T(8,128)(2,1)} async-done(((bf16[16,256,4096]{2,1,0:T(8,128)(2,1)}), bf16[16,256,4096]{2,1,0:T(8,128)(2,1)}, u32[]{:S(2)}, u32[]{:S(2)}) %all-to-all-start.2) | async-done | bytes 33554464 | tf_op jit(solution)/shard_map/all_to_all | solution.py:62
  535.4 4.7 all-to-all-start.1
  544.8 9.1 reduce-window.6
  554.4 3.8 constant_dynamic-slice_fusion.6
  558.3 101.4 %all-to-all-done.1 = bf16[256,16,1024]{2,0,1:T(8,128)(2,1)} async-done(((bf16[256,16,1024]{2,0,1:T(8,128)(2,1)}), bf16[256,16,1024]{2,0,1:T(8,128)(2,1)}, u32[]{:S(2)}, u32[]{:S(2)}) %all-to-all-start.1) | async-done | bytes 8388640 | tf_op jit(solution)/shard_map/all_to_all | solution.py:55
  659.7 6.0 pad_maximum_fusion
  665.7 7.0 collective-permute-start
  673.5 7.5 maximum_maximum_fusion
  681.0 23.0 %multiply_convert_fusion.3 = bf16[4096,1536]{1,0:T(8,128)(2,1)} fusion(bf16[4099,1536]{1,0:T(8,128)(2,1)S(1)} %maximum_maximum_fusion, f32[1536]{0:T(1024)S(1)} %pad_maximum_fusion.1, f32[1536]{0:T(1024)S(1)} %get-tuple-element.255, f32[1536]{0:T(1024)S(1)} %get-tuple-element.256, f32[1536]{0:T(1024)S(1)} %get-tuple-element.257, ...), kind=kLoop, calls=%fused_computation.30 | loop fusion | flops 138412032 | bytes 62945280 | tf_op jit(solution)/shard_map/convert_element_type | solution.py:87
  704.0 7.8 slice.85
  711.8 4.5 fusion.23
  716.2 180.6 %while.29 = (s32[]{:T(128)}, f32[256,1024]{1,0:T(8,128)S(1)}, f32[8,512,1024]{2,1,0:T(8,128)}, f32[8,256,1024]{2,1,0:T(8,128)}, f32[8,512,16]{1,2,0:T(8,128)}, /...) while((s32[]{:T(128)}, f32[256,1024]{1,0:T(8,128)S(1)}, ...), condition=%wide.region_3.4_spmd.clone, body=%wide.region_2.3_spmd.clone.sunk | while | flops 963395584 | bytes 31083584 | solution.py:119
  718.0 2.3 fusion.41
  722.3 7.1 fusion.42
  740.6 2.3 fusion.41
  744.8 7.1 fusion.42
  763.2 2.3 fusion.41
  767.5 7.1 fusion.42
  785.8 2.3 fusion.41
  790.0 7.1 fusion.42
  808.3 2.3 fusion.41
  812.6 7.1 fusion.42
  830.9 2.3 fusion.41
  835.1 7.1 fusion.42
  853.5 2.3 fusion.41
  857.7 7.1 fusion.42
  876.1 2.3 fusion.41
  880.3 7.1 fusion.42
  900.9 13.0 %all-reduce.1 = f32[128]{0:T(128)S(1)} all-reduce(f32[128]{0:T(128)S(1)} %dynamic-update-slice), channel_id=2, replica_groups=mesh['ctx'=8,'head'=16] {'ctx'}, use_global_device_ids=true, to_apply=%add.1 | all-reduce | flops 128 | bytes 1024
  914.4 8.1 broadcast_in_dim.62
  922.4 16.5 %copy.56 = f32[8,512,1024]{2,1,0:T(8,128)} copy(f32[8,512,1024]{1,2,0:T(8,128)} %bitcast.113) | data formatting | bytes 33554432 | tf_op jit(solution)/shard_map/exp | solution.py:135
  938.9 8.9 all-gather.4.cloned.1.call-done
  947.8 18.5 %while.30 = (s32[]{:T(128)}, f32[256,1024]{1,0:T(8,128)S(1)}, s32[]{:T(128)}, f32[8,16]{1,0:T(8,128)S(1)}, f32[8,256,1024]{2,1,0:T(8,128)}, /*index=5*/s32[]{:T(128)}, s32[]{:T(128)}) while((s32[]{:T(128)}, f32[256,1024]{1,0:T(8,128)S(1)}, s32[]{:T(128)}, f32[8,16]{1,0:T(8,128)S(1)}, f32[8,256,1024]{2,1,0:T(8,128)}, ...), condition=%wide.region_7.8_spmd.clone, body=%wide.region_6.7_spmd.clone.sunk | while | flops 1048580 | bytes 3162409 | solution.py:34
  947.9 2.1 fusion.43
  950.3 2.1 fusion.43
  952.6 2.1 fusion.43
  954.9 2.1 fusion.43
  957.2 2.1 fusion.43
  959.5 2.1 fusion.43
  961.8 2.1 fusion.43
  966.3 22.2 %add_convert_fusion = bf16[8,512,1024]{2,1,0:T(8,128)(2,1)} fusion(bf16[8,512,1024]{2,1,0:T(8,128)(2,1)} %get-tuple-element.450, f32[8,512,1024]{2,1,0:T(8,128)} %get-tuple-element.153, f32[8,512,1024]{2,1,0:T(8,128)} %copy.56, bf16[8,512,256]{2,1,0:T(8,128)(2,1)} %bitcast.14, f32[1024]{0:T(1024)S(1)} %mul.190, f32[8,256,1024]{2,1,0:T(8,128)} %get-tuple-element.154, ...), kind=kOutput, calls=%fused_computation.31 | convolution fusion | flops 12914262016 | bytes 61902848 | tf_op jit(solution)/shard_map/bqn,bnc->bqc/dot_general | solution.py:136
  (216 shorter events, 120.8 us)
Async XLA Ops:
  8.2 15.3 %all-to-all-start = ((bf16[256,16,16]{0,2,1:T(8,128)(2,1)}), bf16[256,16,16]{0,2,1:T(8,128)(2,1)S(1)}, u32[]{:S(2)}, u32[]{:S(2)}) async-start(bf16[256,16,16]{0,2,1:T(8,128)(2,1)} %bitcast), calls=%async_computation | async-start | bytes 262144 | tf_op jit(solution)/shard_map/all_to_all | solution.py:56
  34.4 501.0 %all-to-all-start.2 = ((bf16[16,256,4096]{2,1,0:T(8,128)(2,1)}), bf16[16,256,4096]{2,1,0:T(8,128)(2,1)}, u32[]{:S(2)}, u32[]{:S(2)}) async-start(bf16[16,256,4096]{2,1,0:T(8,128)(2,1)} %stack.2), calls=%async_computation.2 | async-start | bytes 67108864 | tf_op jit(solution)/shard_map/all_to_all | solution.py:62
  72.2 468.8 %copy-start.3 = (f32[256]{0:T(256)S(1)}, f32[256]{0:T(256)}, u32[]{:S(2)}) copy-start(f32[256]{0:T(256)} %param.16) | copy-start | bytes 3076
  72.2 468.9 %copy-start.4 = (f32[256]{0:T(256)S(1)}, f32[256]{0:T(256)}, u32[]{:S(2)}) copy-start(f32[256]{0:T(256)} %param.15) | copy-start | bytes 3076
  535.4 124.2 %all-to-all-start.1 = ((bf16[256,16,1024]{2,0,1:T(8,128)(2,1)}), bf16[256,16,1024]{2,0,1:T(8,128)(2,1)}, u32[]{:S(2)}, u32[]{:S(2)}) async-start(bf16[256,16,1024]{2,0,1:T(8,128)(2,1)} %copy.53), calls=%async_computation.1 | async-start | bytes 16777216 | tf_op jit(solution)/shard_map/all_to_all | solution.py:55
  540.2 407.6 %all-gather.4.cloned.1.call-start = ((), (), s32[]{:S(2)}) async-start(), calls=%async_computation.3 | async-start | bytes 9437184 | tf_op jit(solution)/shard_map/all_gather | solution.py:22
  659.7 13.8 %copy-start.2 = (bf16[4096,256]{1,0:T(8,128)(2,1)S(1)}, bf16[4096,256]{1,0:T(8,128)(2,1)}, u32[]{:S(2)}) copy-start(bf16[4096,256]{1,0:T(8,128)(2,1)} %get-tuple-element.291) | copy-start | bytes 6291460
  665.7 7.8 collective-permute-start
  716.2 181.7 %copy-start.5 = (f32[256]{0:T(256)S(1)}, f32[256]{0:T(256)}, u32[]{:S(2)}) copy-start(f32[256]{0:T(256)} %param.17) | copy-start | bytes 3076
  716.2 181.9 %copy-start.6 = (u32[128]{0:T(128)S(1)}, u32[128]{0:T(128)}, u32[]{:S(2)}) copy-start(u32[128]{0:T(128)} %constant.103) | copy-start | bytes 1540
  722.2 7.2 copy-start.1
  744.7 7.2 copy-start.1
  767.4 7.2 copy-start.1
  789.9 7.2 copy-start.1
  812.5 7.2 copy-start.1
  835.0 7.2 copy-start.1
  857.6 7.2 copy-start.1
  880.2 7.2 copy-start.1
  896.9 1.0 copy-start
Sparse Core Ops, SparseCore 0:
  898.0 49.7 all-gather.3
